TPU v7x, 512 devices: a whole 4x8x8 slice. The times are simulated.
512 devices in a mesh: section: 8 (over z), ctx: 8 (over y_hi, x), tp: 8 (over y_lo, core).
Axes of the slice: x: 4, y: 8 (y_hi: 2, y_lo: 4; y = y_hi * 4 + y_lo), z: 8, core: 2. Of those that a mesh axis runs over, the one named last changes fastest.
Arguments:
- block_order: int32 [16], replicated, may hold values from 0 to 15, each once
- plan: int32 [8], replicated, may hold values from 0 to 1
- q_box: bfloat16 [8, 2, 1408, 8192], P('section', None, 'ctx', 'tp'), may hold values from -8 to 8
- k_box: bfloat16 [8, 2, 1408, 1024], P('section', None, ('ctx', 'tp')), may hold values from -8 to 8
- v_box: bfloat16 [8, 2, 1408, 1024], P('section', None, ('ctx', 'tp')), may hold values from -6 to 6
- grad_out: bfloat16 [8, 1408, 8192], P('section', 'ctx', 'tp'), may hold values from -6 to 6
Outputs:
- attn_out: bfloat16 [8, 1408, 8192], P('section', 'ctx', 'tp')
- grad_q: bfloat16 [8, 1408, 8192], P('section', 'ctx', 'tp')
- grad_k: float32 [8, 1408, 1024], P('section', ('ctx', 'tp'))
- grad_v: float32 [8, 1408, 1024], P('section', ('ctx', 'tp'))
Inputs may be any that keep to these rules, and one draw needn't show every extreme that they name: `block_order`: a permutation: every block sits in exactly one storage slot, slot j covering storage rows j * 88 to (j + 1) * 88 - 1.
All inputs are finite; a program needn't handle non-finite values.
Results may differ from a plain program's by a relative error of at most 0.012.
Values may be sent and summed in bfloat16 or wider, within the bound.
No kernel may reach another device: no remote copies, remote signals or barrier semaphores. Data moves between devices by JAX's collectives and lax.ppermute only.
A program may use at most 64 MiB of HBM per device.

v0:
```python
import jax
import jax.numpy as jnp
from jax import lax
from jax.sharding import PartitionSpec as P

HEAD_DIM = 128
NEG = -1e30


def passed_along(block, axis, distance):
    devices = range(lax.axis_size(axis))
    route = [((i - distance) % len(devices), i) for i in devices]
    return lax.ppermute(block, axis, route)


def body(block_order, plan, q_box, k_box, v_box, grad_out):
    tp_count = lax.axis_size("tp")
    ctx_count = lax.axis_size("ctx")
    section_count = lax.axis_size("section")
    tok_rows = q_box.shape[2]
    kv_rows = k_box.shape[2]
    seq_rows = tok_rows * ctx_count
    block_len = seq_rows // block_order.shape[0]
    head_size = HEAD_DIM
    heads_local = q_box.shape[3] // head_size
    kv_local = k_box.shape[3] // head_size // tp_count
    group = heads_local // kv_local
    kv_width = kv_local * head_size
    scale = head_size ** (-0.5)
    section_rank = lax.axis_index("section")
    receiver = (section_rank + 1) % section_count
    wanted = lax.dynamic_index_in_dim(plan, receiver, 0, keepdims=False)
    q_send = lax.dynamic_index_in_dim(q_box[0], wanted, 0, keepdims=False)
    k_send = lax.dynamic_index_in_dim(k_box[0], wanted, 0, keepdims=False)
    v_send = lax.dynamic_index_in_dim(v_box[0], wanted, 0, keepdims=False)
    kv_send = jnp.stack(
        [k_send.reshape(kv_rows, -1, head_size), v_send.reshape(kv_rows, -1, head_size)], axis=2
    ).reshape(kv_rows, -1)
    queries, kv_rows_in = passed_along((q_send, kv_send), "section", 1)
    cotangent = passed_along(grad_out[0], "section", -1)
    kv_tok = lax.all_to_all(kv_rows_in, "tp", split_axis=1, concat_axis=0, tiled=True)
    kv_full = lax.all_gather(kv_tok, "ctx", axis=0, tiled=True)
    kv_full = kv_full.reshape(seq_rows, kv_local, 2, head_size)
    key_heads = kv_full[:, :, 0, :]
    value_heads = kv_full[:, :, 1, :]
    positions = (
        block_order[:, None] * block_len + jnp.arange(block_len, dtype=jnp.int32)[None, :]
    ).reshape(seq_rows)
    query_pos = lax.dynamic_slice_in_dim(positions, lax.axis_index("ctx") * tok_rows, tok_rows)
    visible = (positions[None, :] <= query_pos[:, None])[None, None]
    q4 = queries.reshape(tok_rows, kv_local, group, head_size)
    do4 = cotangent.reshape(tok_rows, kv_local, group, head_size)
    scores = jnp.einsum("qgjd,kgd->gjqk", q4, key_heads, preferred_element_type=jnp.float32) * scale
    scores = jnp.where(visible, scores, NEG)
    top_score = jnp.max(scores, axis=-1, keepdims=True)
    totals = jnp.sum(jnp.where(visible, jnp.exp(scores - top_score), 0.0), axis=-1, keepdims=True)
    log_total = top_score + jnp.log(totals)
    probs = jnp.where(visible, jnp.exp(scores - log_total), 0.0)
    probs_low = probs.astype(jnp.bfloat16)
    attended = jnp.einsum(
        "gjqk,kgd->qgjd", probs_low, value_heads, preferred_element_type=jnp.float32
    )
    delta = jnp.sum(do4.astype(jnp.float32) * attended, axis=-1)
    dprobs = jnp.einsum("qgjd,kgd->gjqk", do4, value_heads, preferred_element_type=jnp.float32)
    dscores = (probs * (dprobs - jnp.transpose(delta, (1, 2, 0))[..., None])).astype(jnp.bfloat16)
    q_grad = (
        jnp.einsum("gjqk,kgd->qgjd", dscores, key_heads, preferred_element_type=jnp.float32) * scale
    ).astype(jnp.bfloat16)
    key_grad = jnp.einsum("gjqk,qgjd->kgd", dscores, q4, preferred_element_type=jnp.float32) * scale
    value_grad = jnp.einsum("gjqk,qgjd->kgd", probs_low, do4, preferred_element_type=jnp.float32)
    attended_flat = attended.astype(jnp.bfloat16).reshape(tok_rows, heads_local * head_size)
    q_grad_flat = q_grad.reshape(tok_rows, heads_local * head_size)
    grad_terms = jnp.stack([key_grad, value_grad], axis=2).reshape(seq_rows, 2 * kv_width)
    own_grads = lax.psum_scatter(grad_terms, "ctx", scatter_dimension=0, tiled=True)
    tok_grads = lax.all_to_all(own_grads, "tp", split_axis=0, concat_axis=1, tiled=True)
    tok_grads = tok_grads.reshape(kv_rows, -1, 2, head_size)
    k_grad_tokens = tok_grads[:, :, 0, :].reshape(kv_rows, -1)
    v_grad_tokens = tok_grads[:, :, 1, :].reshape(kv_rows, -1)
    return (attended_flat[None], q_grad_flat[None], k_grad_tokens[None], v_grad_tokens[None])


def solution(mesh):
    in_specs = (
        P(),
        P(),
        P("section", None, "ctx", "tp"),
        P("section", None, ("ctx", "tp"), None),
        P("section", None, ("ctx", "tp"), None),
        P("section", "ctx", "tp"),
    )
    out_specs = (
        P("section", "ctx", "tp"),
        P("section", "ctx", "tp"),
        P("section", ("ctx", "tp"), None),
        P("section", ("ctx", "tp"), None),
    )
    return jax.shard_map(body, mesh=mesh, in_specs=in_specs, out_specs=out_specs, check_vma=False)
```

profile of v0, /device:TPU:1, one launch (start us, length us, event | category | flops | bytes accessed | tf_op | source)
XLA Modules:
  0.0 212.7 jit_solution(3541561579943129193)
XLA Ops:
  7.2 0.0 copy-start
  7.2 11.6 %collective-permute-start.2 = (bf16[176,1024]{1,0:T(8,128)(2,1)}, bf16[176,1024]{1,0:T(8,128)(2,1)S(1)}, u32[]{:S(2)}, u32[]{:S(2)}) collective-permute-start(bf16[176,1024]{1,0:T(8,128)(2,1)} %bitcast.163), channel_id=1, source_target_pairs={{64,0},{128,64},{192,128},{256,192},{320,256},{384,320},{448,384},... | collective-permute-start | bytes 1081352 | tf_op jit(solution)/shard_map/ppermute | solution.py:13
  18.8 1.2 dynamic_slice.18
  22.0 1.5 dynamic-slice_reduce_fusion
  23.6 0.1 copy.26
  23.7 1.9 collective-permute-start
  25.6 0.0 copy-done
  25.6 0.8 dynamic-slice_bitcast_fusion
  26.4 1.9 collective-permute-start.1
  28.3 0.7 broadcast_multiply_fusion
  29.0 0.1 iota_add_fusion
  29.1 0.1 add.59
  29.1 0.1 dynamic_slice.21
  29.2 1.0 collective-permute-done
  30.3 0.7 copy.27
  31.0 7.0 %all-to-all-start = ((bf16[22,8,256]{2,0,1:T(8,128)(2,1)}), bf16[22,8,256]{2,0,1:T(8,128)(2,1)S(1)}, u32[]{:S(2)}, u32[]{:S(2)}) async-start(bf16[22,8,256]{2,0,1:T(8,128)(2,1)} %copy.27), calls=%async_computation | async-start | bytes 196608 | tf_op jit(solution)/shard_map/all_to_all | solution.py:41
  37.9 0.0 reduce-scatter.2.cloned.1.call-start
  37.9 0.2 broadcast_compare_fusion
  38.2 5.1 %all-to-all-done = bf16[22,8,256]{2,0,1:T(8,128)(2,1)S(1)} async-done(((bf16[22,8,256]{2,0,1:T(8,128)(2,1)}), bf16[22,8,256]{2,0,1:T(8,128)(2,1)S(1)}, u32[]{:S(2)}, u32[]{:S(2)}) %all-to-all-start) | async-done | bytes 90144 | tf_op jit(solution)/shard_map/all_to_all | solution.py:41
  43.3 41.5 %all_gather.3 = bf16[1408,256]{1,0:T(8,128)(2,1)S(1)} all-gather(bf16[176,256]{1,0:T(8,128)(2,1)S(1)} %all_to_all.29), channel_id=1, replica_groups=mesh['section'=8,'ctx'=8,'tp'=8] {'ctx'}, dimensions={0}, use_global_device_ids=true | all-gather | bytes 811008 | tf_op jit(solution)/shard_map/all_gather | solution.py:42
  84.9 0.3 copy.28
  85.2 0.0 collective-permute-done.2
  85.2 0.1 convert_bitcast_fusion
  85.3 0.1 copy.47
  85.4 0.0 collective-permute-done.1
  85.4 2.0 fusion.30
  87.4 2.0 select_reduce_fusion
  89.4 0.1 copy.48
  89.5 1.8 fusion.18
  91.3 2.7 %fusion.6 = bf16[8,176,1408]{2,1,0:T(8,128)(2,1)S(1)} fusion(f32[8,176]{1,0:T(8,128)S(1)} %bitcast.162, f32[1,8,176,1408]{3,2,1,0:T(8,128)S(1)} %get-tuple-element.13, f32[8,176]{1,0:T(8,128)S(1)} %log_add_fusion, pred[176,1408]{1,0:T(8,128)(4,1)S(1)} %broadcast_compare_fusion, bf16[1408,1,2,128]{0,3,2,1:T(8,128)(2,1)S(1)} %bitcast.146, ...), kind=kOutput, calls=%fused_computation.10 | convolution fusion | flops 517423104 | bytes 12879872 | tf_op jit(solution)/shard_map/qgjd,kgd->gjqk/dot_general | solution.py:64
  94.0 0.0 copy-start.1
  94.0 0.9 fusion.13
  94.9 1.7 convolution_bitcast_fusion
  96.6 0.0 copy-done.1
  96.6 0.1 pad_maximum_fusion
  96.7 1.5 copy.38
  98.2 0.0 reduce-scatter.2.cloned.1.call-update
  98.2 0.1 copy.32
  98.3 0.9 broadcast_in_dim_reshape.7
  99.2 90.8 %reduce-scatter.2.cloned.1.call-done = f32[176,256]{1,0:T(8,128)} async-done(((f32[1408,256]{1,0:T(8,128)}), f32[176,256]{1,0:T(8,128)}) %reduce-scatter.2.cloned.1.call-update) | async-done | bytes 180240 | tf_op jit(solution)/shard_map/reduce_scatter | solution.py:74
  190.0 1.6 all_to_all.30
  191.6 7.0 %all-to-all-start.1 = ((f32[8,22,256]{2,1,0:T(8,128)}), f32[8,22,256]{2,1,0:T(8,128)S(1)}, u32[]{:S(2)}, u32[]{:S(2)}) async-start(f32[8,22,256]{2,1,0:T(8,128)} %all_to_all.30), calls=%async_computation.2 | async-start | bytes 393216 | tf_op jit(solution)/shard_map/all_to_all | solution.py:75
  198.6 3.3 %fusion.17 = bf16[176,1,8,128]{3,0,2,1:T(8,128)(2,1)S(1)} fusion(bf16[8,176,1408]{2,1,0:T(8,128)(2,1)} %copy-done.1, bf16[1408,1,2,128]{0,3,2,1:T(8,128)(2,1)S(1)} %bitcast.147), kind=kOutput, calls=%fused_computation.19 | convolution fusion | flops 507871232 | bytes 4685824 | tf_op jit(solution)/shard_map/gjqk,kgd->qgjd/dot_general | solution.py:67
  201.9 0.1 copy.35
  202.0 0.9 broadcast_in_dim_reshape.8
  202.9 2.2 %all-to-all-done.1 = f32[8,22,256]{2,1,0:T(8,128)S(1)} async-done(((f32[8,22,256]{2,1,0:T(8,128)}), f32[8,22,256]{2,1,0:T(8,128)S(1)}, u32[]{:S(2)}, u32[]{:S(2)}) %all-to-all-start.1) | async-done | bytes 180256 | tf_op jit(solution)/shard_map/all_to_all | solution.py:75
  205.1 0.1 copy.75
  205.2 0.7 fusion.29
  (10 shorter events, 0.1 us)
Async XLA Ops:
  7.2 18.5 %copy-start = (bf16[1,2,176,1024]{3,2,1,0:T(8,128)(2,1)S(1)}, bf16[1,2,176,1024]{3,2,1,0:T(8,128)(2,1)}, u32[]{:S(2)}) copy-start(bf16[1,2,176,1024]{3,2,1,0:T(8,128)(2,1)} %param.8) | copy-start | bytes 2162692
  7.2 78.0 %collective-permute-start.2 = (bf16[176,1024]{1,0:T(8,128)(2,1)}, bf16[176,1024]{1,0:T(8,128)(2,1)S(1)}, u32[]{:S(2)}, u32[]{:S(2)}) collective-permute-start(bf16[176,1024]{1,0:T(8,128)(2,1)} %bitcast.163), channel_id=1, source_target_pairs={{64,0},{128,64},{192,128},{256,192},{320,256},{384,320},{448,384},... | collective-permute-start | bytes 1081352 | tf_op jit(solution)/shard_map/ppermute | solution.py:13
  23.7 6.6 %collective-permute-start = (bf16[22,2048]{1,0:T(8,128)(2,1)S(1)}, bf16[22,2048]{1,0:T(8,128)(2,1)S(1)}, u32[]{:S(2)}, u32[]{:S(2)}) collective-permute-start(bf16[22,2048]{1,0:T(8,128)(2,1)S(1)} %reshape.167), channel_id=1, source_target_pairs={{448,0},{0,64},{64,128},{128,192},{192,256},{256,320},{320,384},{3... | collective-permute-start | bytes 270344 | tf_op jit(solution)/shard_map/ppermute | solution.py:13
  26.4 59.0 %collective-permute-start.1 = (bf16[176,1024]{1,0:T(8,128)(2,1)}, bf16[176,1024]{1,0:T(8,128)(2,1)S(1)}, u32[]{:S(2)}, u32[]{:S(2)}) collective-permute-start(bf16[176,1024]{1,0:T(8,128)(2,1)} %dynamic-slice_bitcast_fusion), channel_id=1, source_target_pairs={{448,0},{0,64},{64,128},{128,192},{192,256},{256,320},{320,384},{3... | collective-permute-start | bytes 1081352 | tf_op jit(solution)/shard_map/ppermute | solution.py:13
  31.0 12.3 %all-to-all-start = ((bf16[22,8,256]{2,0,1:T(8,128)(2,1)}), bf16[22,8,256]{2,0,1:T(8,128)(2,1)S(1)}, u32[]{:S(2)}, u32[]{:S(2)}) async-start(bf16[22,8,256]{2,0,1:T(8,128)(2,1)} %copy.27), calls=%async_computation | async-start | bytes 196608 | tf_op jit(solution)/shard_map/all_to_all | solution.py:41
  37.9 152.1 %reduce-scatter.2.cloned.1.call-start = ((), (), s32[]{:S(2)}) async-start(), calls=%async_computation.3 | async-start | bytes 1622016 | tf_op jit(solution)/shard_map/reduce_scatter | solution.py:74
  94.0 2.6 %copy-start.1 = (bf16[8,176,1408]{2,1,0:T(8,128)(2,1)}, bf16[8,176,1408]{2,1,0:T(8,128)(2,1)S(1)}, u32[]{:S(2)}) copy-start(bf16[8,176,1408]{2,1,0:T(8,128)(2,1)S(1)} %fusion.6) | copy-start | bytes 11894788
  191.6 13.5 %all-to-all-start.1 = ((f32[8,22,256]{2,1,0:T(8,128)}), f32[8,22,256]{2,1,0:T(8,128)S(1)}, u32[]{:S(2)}, u32[]{:S(2)}) async-start(f32[8,22,256]{2,1,0:T(8,128)} %all_to_all.30), calls=%async_computation.2 | async-start | bytes 393216 | tf_op jit(solution)/shard_map/all_to_all | solution.py:75
Sparse Core Ops, SparseCore 0:
  98.4 91.6 reduce-scatter.1
where the time goes:
time: 213 us
  waiting for transfers between devices  99.2 us (47%)
  blocking collectives  41.5 us (19%)
  starting transfers between devices  29.4 us (14%)
  between operations  16.2 us (8%)
  matrix products  12.3 us (6%)
  local copies, waits for them, and re-layouts  10.9 us (5%)
  other arithmetic  3.13 us (1%)
    reduce_scatter x1, waiting for transfers between devices, body(): lax.psum_scatter(grad_terms, 'ctx', scatter_dimension=0, tiled=True)  90.8 us
    all_gather x1, blocking collectives, body(): kv_full = lax.all_gather(kv_tok, 'ctx', axis=0, tiled=True)  41.5 us
    ppermute x3, starting transfers between devices, passed_along(): return lax.ppermute(block, axis, route)  15.4 us
    all_to_all x1, starting transfers between devices, body(): lax.all_to_all(kv_rows_in, 'tp', split_axis=1, concat_axis=0, tiled=True)  6.98 us
    all_to_all x1, starting transfers between devices, body(): lax.all_to_all(own_grads, 'tp', split_axis=0, concat_axis=1, tiled=True)  6.96 us
    all_to_all x1, waiting for transfers between devices, body(): lax.all_to_all(kv_rows_in, 'tp', split_axis=1, concat_axis=0, tiled=True)  5.15 us
  transfers between devices with their start and end apart: 6, of which 4 were waited for; matrix products, arithmetic and copies ran while one was open for 5% of the time, Pallas kernels for 0%

commit v1 on v0

--- a/solution.py
+++ b/solution.py
@@ -39,7 +39,9 @@
     queries, kv_rows_in = passed_along((q_send, kv_send), "section", 1)
     cotangent = passed_along(grad_out[0], "section", -1)
     kv_tok = lax.all_to_all(kv_rows_in, "tp", split_axis=1, concat_axis=0, tiled=True)
-    kv_full = lax.all_gather(kv_tok, "ctx", axis=0, tiled=True)
+    kv_full = jnp.concatenate(
+        lax.all_to_all(jnp.stack([kv_tok] * lax.axis_size("ctx")), "ctx", 0, 0), axis=0
+    )
     kv_full = kv_full.reshape(seq_rows, kv_local, 2, head_size)
     key_heads = kv_full[:, :, 0, :]
     value_heads = kv_full[:, :, 1, :]

time: 213 us -> 192 us (0.901)
  blocking collectives: 41.5 us -> 0 us
  waiting for transfers between devices: 99.2 us -> 114 us
  local copies, waits for them, and re-layouts: 10.9 us -> 13.9 us
    all_gather x1 -> x0, blocking collectives: 41.5 us -> none  [body(): kv_full = lax.all_gather(kv_tok, 'ctx', axis=0, tiled=True)]
    ppermute x3, waiting for transfers between devices: 1.04 us -> 16.9 us  [passed_along(): return lax.ppermute(block, axis, route)]
    all_to_all x0 -> x1, starting transfers between devices: none -> 7.71 us  [body(): lax.all_to_all(jnp.stack([kv_tok] * lax.axis_size('ctx')), 'ctx', 0, 0)]
    ppermute x3, starting transfers between devices: 15.4 us -> 10.2 us  [passed_along(): return lax.ppermute(block, axis, route)]
    all_to_all x1, waiting for transfers between devices: 5.15 us -> 1.92 us  [body(): lax.all_to_all(kv_rows_in, 'tp', split_axis=1, concat_axis=0, tiled=True)]
    all_to_all x0 -> x1, waiting for transfers between devices: none -> 3.15 us  [body(): lax.all_to_all(jnp.stack([kv_tok] * lax.axis_size('ctx')), 'ctx', 0, 0)]
  transfers between devices with their start and end apart: 6 -> 7, of which waited for: 4 -> 6; matrix products, arithmetic and copies ran while one was open for 5% -> 5% of each run, Pallas kernels for 0% -> 0%
where the time goes in v1:
time: 192 us; the launch traced here: 191 us
  waiting for transfers between devices  114 us (59%)
  starting transfers between devices  31 us (16%)
  between operations  16.3 us (8%)
  local copies, waits for them, and re-layouts  13.9 us (7%)
  matrix products  13.1 us (7%)
  other arithmetic  3.21 us (2%)
    reduce_scatter x1, waiting for transfers between devices, body(): lax.psum_scatter(grad_terms, 'ctx', scatter_dimension=0, tiled=True)  89.8 us
    ppermute x3, waiting for transfers between devices, passed_along(): return lax.ppermute(block, axis, route)  16.9 us
    ppermute x3, starting transfers between devices, passed_along(): return lax.ppermute(block, axis, route)  10.2 us
    all_to_all x1, starting transfers between devices, body(): lax.all_to_all(jnp.stack([kv_tok] * lax.axis_size('ctx')), 'ctx', 0, 0)  7.71 us
    all_to_all x1, starting transfers between devices, body(): lax.all_to_all(own_grads, 'tp', split_axis=0, concat_axis=1, tiled=True)  6.96 us
    all_to_all x1, starting transfers between devices, body(): lax.all_to_all(kv_rows_in, 'tp', split_axis=1, concat_axis=0, tiled=True)  6.12 us
  transfers between devices with their start and end apart: 7, of which 6 were waited for; matrix products, arithmetic and copies ran while one was open for 5% of the time, Pallas kernels for 0%

profile of v1, /device:TPU:1, one launch (start us, length us, event | category | flops | bytes accessed | tf_op | source)
XLA Modules:
  0.0 191.5 jit_solution(5629588958024853475)
XLA Ops:
  7.2 0.0 copy-start
  7.2 1.3 dynamic_slice.18
  10.4 1.5 dynamic-slice_reduce_fusion
  12.0 0.1 copy.25
  12.1 4.8 %collective-permute-start = (bf16[22,2048]{1,0:T(8,128)(2,1)S(1)}, bf16[22,2048]{1,0:T(8,128)(2,1)S(1)}, u32[]{:S(2)}, u32[]{:S(2)}) collective-permute-start(bf16[22,2048]{1,0:T(8,128)(2,1)S(1)} %reshape.167), channel_id=1, source_target_pairs={{448,0},{0,64},{64,128},{128,192},{192,256},{256,320},{320,384},{3... | collective-permute-start | bytes 270344 | tf_op jit(solution)/shard_map/ppermute | solution.py:13
  17.0 9.2 %collective-permute-done = bf16[22,2048]{1,0:T(8,128)(2,1)S(1)} collective-permute-done((bf16[22,2048]{1,0:T(8,128)(2,1)S(1)}, bf16[22,2048]{1,0:T(8,128)(2,1)S(1)}, u32[]{:S(2)}, u32[]{:S(2)}) %collective-permute-start) | collective-permute-done | bytes 90144 | tf_op jit(solution)/shard_map/ppermute | solution.py:13
  26.1 0.7 copy.26
  26.8 6.1 %all-to-all-start = ((bf16[22,8,256]{2,0,1:T(8,128)(2,1)}), bf16[22,8,256]{2,0,1:T(8,128)(2,1)S(1)}, u32[]{:S(2)}, u32[]{:S(2)}) async-start(bf16[22,8,256]{2,0,1:T(8,128)(2,1)} %copy.26), calls=%async_computation | async-start | bytes 196608 | tf_op jit(solution)/shard_map/all_to_all | solution.py:41
  32.9 3.4 %collective-permute-start.2 = (bf16[176,1024]{1,0:T(8,128)(2,1)}, bf16[176,1024]{1,0:T(8,128)(2,1)S(1)}, u32[]{:S(2)}, u32[]{:S(2)}) collective-permute-start(bf16[176,1024]{1,0:T(8,128)(2,1)} %bitcast.154), channel_id=1, source_target_pairs={{64,0},{128,64},{192,128},{256,192},{320,256},{384,320},{448,384},... | collective-permute-start | bytes 1081352 | tf_op jit(solution)/shard_map/ppermute | solution.py:13
  36.4 1.9 %all-to-all-done = bf16[22,8,256]{2,0,1:T(8,128)(2,1)S(1)} async-done(((bf16[22,8,256]{2,0,1:T(8,128)(2,1)}), bf16[22,8,256]{2,0,1:T(8,128)(2,1)S(1)}, u32[]{:S(2)}, u32[]{:S(2)}) %all-to-all-start) | async-done | bytes 90144 | tf_op jit(solution)/shard_map/all_to_all | solution.py:41
  38.3 0.9 stack.27
  39.3 7.7 %all-to-all-start.1 = ((bf16[8,176,256]{2,1,0:T(8,128)(2,1)}), bf16[8,176,256]{2,1,0:T(8,128)(2,1)S(1)}, u32[]{:S(2)}, u32[]{:S(2)}) async-start(bf16[8,176,256]{2,1,0:T(8,128)(2,1)} %stack.27), calls=%async_computation.1 | async-start | bytes 1441792 | tf_op jit(solution)/shard_map/all_to_all | solution.py:43
  47.0 0.0 reduce-scatter.2.cloned.1.call-start
  47.0 0.0 copy-done
  47.1 1.9 %collective-permute-start.1 = (bf16[176,1024]{1,0:T(8,128)(2,1)S(1)}, bf16[176,1024]{1,0:T(8,128)(2,1)S(1)}, u32[]{:S(2)}, u32[]{:S(2)}) collective-permute-start(bf16[176,1024]{1,0:T(8,128)(2,1)S(1)} %dynamic-slice_bitcast_fusion), channel_id=1, source_target_pairs={{448,0},{0,64},{64,128},{128,192},{192,256},{256,320},{320,384},{3... | collective-permute-start | bytes 1081352 | tf_op jit(solution)/shard_map/ppermute | solution.py:13
  49.0 0.7 broadcast_multiply_fusion
  49.7 0.1 iota_add_fusion
  49.7 0.1 add.59
  49.8 0.1 dynamic_slice.21
  49.9 0.2 broadcast_compare_fusion
  50.1 0.0 collective-permute-done.2
  50.1 0.1 convert_bitcast_fusion
  50.2 1.0 copy.45
  51.2 7.7 %collective-permute-done.1 = bf16[176,1024]{1,0:T(8,128)(2,1)S(1)} collective-permute-done((bf16[176,1024]{1,0:T(8,128)(2,1)S(1)}, bf16[176,1024]{1,0:T(8,128)(2,1)S(1)}, u32[]{:S(2)}, u32[]{:S(2)}) %collective-permute-start.1) | collective-permute-done | bytes 360480 | tf_op jit(solution)/shard_map/ppermute | solution.py:13
  58.9 0.1 copy.46
  59.0 3.1 %all-to-all-done.1 = bf16[8,176,256]{2,1,0:T(8,128)(2,1)S(1)} async-done(((bf16[8,176,256]{2,1,0:T(8,128)(2,1)}), bf16[8,176,256]{2,1,0:T(8,128)(2,1)S(1)}, u32[]{:S(2)}, u32[]{:S(2)}) %all-to-all-start.1) | async-done | bytes 720928 | tf_op jit(solution)/shard_map/all_to_all | solution.py:43
  62.1 0.2 reshape_reshape.3
  62.3 1.1 fusion.29
  63.3 0.0 copy-start.2
  63.4 1.9 fusion.31
  65.3 2.0 %select_reduce_fusion = f32[8,176]{1,0:T(8,128)S(1)} fusion(f32[1,8,176,1408]{3,2,1,0:T(8,128)S(1)} %get-tuple-element.15, f32[8,176]{1,0:T(8,128)S(1)} %get-tuple-element.14, pred[176,1408]{1,0:T(8,128)(4,1)S(1)} %broadcast_compare_fusion), kind=kLoop, calls=%fused_computation.5 | loop fusion | flops 5945984 | bytes 8188928 | tf_op jit(solution)/shard_map/reduce_sum | solution.py:58
  67.3 0.0 copy-done.2
  67.3 2.5 %fusion.18 = (f32[176,8]{0,1:T(8,128)S(1)}, bf16[176,1,8,128]{3,0,2,1:T(8,128)(2,1)}) fusion(f32[176,1,8,128]{3,2,0,1:T(8,128)S(1)} %bitcast.141, f32[1,8,176,1408]{3,2,1,0:T(8,128)S(1)} %get-tuple-element.15, f32[8,176]{1,0:T(8,128)S(1)} %log_add_fusion, pred[176,1408]{1,0:T(8,128)(4,1)S(1)} %broadcast_compare_fusion, ...), kind=kOutput, calls=%fused_computation.21 | convolution fusion | flops 513997440 | bytes 9630720 | tf_op jit(solution)/shard_map/gjqk,kgd->qgjd/dot_general | solution.py:62
  69.8 2.9 %fusion.6 = bf16[8,176,1408]{2,1,0:T(8,128)(2,1)S(1)} fusion(f32[8,176]{1,0:T(8,128)S(1)} %bitcast.153, f32[1,8,176,1408]{3,2,1,0:T(8,128)S(1)} %get-tuple-element.15, f32[8,176]{1,0:T(8,128)S(1)} %log_add_fusion, pred[176,1408]{1,0:T(8,128)(4,1)S(1)} %broadcast_compare_fusion, bf16[1408,1,1,128]{3,2,0,1:T(2,128)(2,1)S(1)} %get-tuple-element.10, ...), kind=kOutput, calls=%fused_computation.10 | convolution fusion | flops 517423104 | bytes 12874752 | tf_op jit(solution)/shard_map/qgjd,kgd->gjqk/dot_general | solution.py:66
  72.7 0.0 copy-start.1
  72.7 0.9 fusion.13
  73.6 1.7 convolution_bitcast_fusion
  75.2 0.0 copy-done.1
  75.3 0.2 pad_maximum_fusion
  75.4 1.5 copy.36
  77.0 0.0 reduce-scatter.2.cloned.1.call-update
  77.0 1.1 copy.30
  78.1 0.9 broadcast_in_dim_reshape.7
  79.0 89.8 %reduce-scatter.2.cloned.1.call-done = f32[176,256]{1,0:T(8,128)} async-done(((f32[1408,256]{1,0:T(8,128)}), f32[176,256]{1,0:T(8,128)}) %reduce-scatter.2.cloned.1.call-update) | async-done | bytes 180240 | tf_op jit(solution)/shard_map/reduce_scatter | solution.py:76
  168.7 1.6 all_to_all.31
  170.4 7.0 %all-to-all-start.2 = ((f32[8,22,256]{2,1,0:T(8,128)}), f32[8,22,256]{2,1,0:T(8,128)S(1)}, u32[]{:S(2)}, u32[]{:S(2)}) async-start(f32[8,22,256]{2,1,0:T(8,128)} %all_to_all.31), calls=%async_computation.3 | async-start | bytes 393216 | tf_op jit(solution)/shard_map/all_to_all | solution.py:77
  177.3 3.3 %fusion.17 = bf16[176,1,8,128]{3,0,2,1:T(8,128)(2,1)S(1)} fusion(bf16[8,176,1408]{2,1,0:T(8,128)(2,1)} %copy-done.1, bf16[1408,1,1,128]{3,2,0,1:T(2,128)(2,1)S(1)} %get-tuple-element.11), kind=kOutput, calls=%fused_computation.19 | convolution fusion | flops 507871232 | bytes 4685824 | tf_op jit(solution)/shard_map/gjqk,kgd->qgjd/dot_general | solution.py:69
  180.7 0.1 copy.33
  180.8 0.9 broadcast_in_dim_reshape.8
  181.6 2.2 %all-to-all-done.2 = f32[8,22,256]{2,1,0:T(8,128)S(1)} async-done(((f32[8,22,256]{2,1,0:T(8,128)}), f32[8,22,256]{2,1,0:T(8,128)S(1)}, u32[]{:S(2)}, u32[]{:S(2)}) %all-to-all-start.2) | async-done | bytes 180256 | tf_op jit(solution)/shard_map/all_to_all | solution.py:77
  183.9 0.1 copy.83
  183.9 0.7 fusion.30
  (11 shorter events, 0.2 us)
Async XLA Ops:
  7.2 39.8 %copy-start = (bf16[1,2,176,1024]{3,2,1,0:T(8,128)(2,1)S(1)}, bf16[1,2,176,1024]{3,2,1,0:T(8,128)(2,1)}, u32[]{:S(2)}) copy-start(bf16[1,2,176,1024]{3,2,1,0:T(8,128)(2,1)} %param.8) | copy-start | bytes 2162692
  12.1 14.0 %collective-permute-start = (bf16[22,2048]{1,0:T(8,128)(2,1)S(1)}, bf16[22,2048]{1,0:T(8,128)(2,1)S(1)}, u32[]{:S(2)}, u32[]{:S(2)}) collective-permute-start(bf16[22,2048]{1,0:T(8,128)(2,1)S(1)} %reshape.167), channel_id=1, source_target_pairs={{448,0},{0,64},{64,128},{128,192},{192,256},{256,320},{320,384},{3... | collective-permute-start | bytes 270344 | tf_op jit(solution)/shard_map/ppermute | solution.py:13
  26.8 11.5 %all-to-all-start = ((bf16[22,8,256]{2,0,1:T(8,128)(2,1)}), bf16[22,8,256]{2,0,1:T(8,128)(2,1)S(1)}, u32[]{:S(2)}, u32[]{:S(2)}) async-start(bf16[22,8,256]{2,0,1:T(8,128)(2,1)} %copy.26), calls=%async_computation | async-start | bytes 196608 | tf_op jit(solution)/shard_map/all_to_all | solution.py:41
  32.9 17.2 %collective-permute-start.2 = (bf16[176,1024]{1,0:T(8,128)(2,1)}, bf16[176,1024]{1,0:T(8,128)(2,1)S(1)}, u32[]{:S(2)}, u32[]{:S(2)}) collective-permute-start(bf16[176,1024]{1,0:T(8,128)(2,1)} %bitcast.154), channel_id=1, source_target_pairs={{64,0},{128,64},{192,128},{256,192},{320,256},{384,320},{448,384},... | collective-permute-start | bytes 1081352 | tf_op jit(solution)/shard_map/ppermute | solution.py:13
  39.3 22.9 %all-to-all-start.1 = ((bf16[8,176,256]{2,1,0:T(8,128)(2,1)}), bf16[8,176,256]{2,1,0:T(8,128)(2,1)S(1)}, u32[]{:S(2)}, u32[]{:S(2)}) async-start(bf16[8,176,256]{2,1,0:T(8,128)(2,1)} %stack.27), calls=%async_computation.1 | async-start | bytes 1441792 | tf_op jit(solution)/shard_map/all_to_all | solution.py:43
  47.0 121.8 %reduce-scatter.2.cloned.1.call-start = ((), (), s32[]{:S(2)}) async-start(), calls=%async_computation.4 | async-start | bytes 1622016 | tf_op jit(solution)/shard_map/reduce_scatter | solution.py:76
  47.1 11.8 %collective-permute-start.1 = (bf16[176,1024]{1,0:T(8,128)(2,1)S(1)}, bf16[176,1024]{1,0:T(8,128)(2,1)S(1)}, u32[]{:S(2)}, u32[]{:S(2)}) collective-permute-start(bf16[176,1024]{1,0:T(8,128)(2,1)S(1)} %dynamic-slice_bitcast_fusion), channel_id=1, source_target_pairs={{448,0},{0,64},{64,128},{128,192},{192,256},{256,320},{320,384},{3... | collective-permute-start | bytes 1081352 | tf_op jit(solution)/shard_map/ppermute | solution.py:13
  63.3 3.9 %copy-start.2 = (f32[22,8,8,128]{3,2,1,0:T(8,128)S(1)}, f32[22,8,8,128]{3,2,1,0:T(8,128)}, u32[]{:S(2)}) copy-start(f32[22,8,8,128]{3,2,1,0:T(8,128)} %copy.45) | copy-start | bytes 2162692
  72.7 2.6 %copy-start.1 = (bf16[8,176,1408]{2,1,0:T(8,128)(2,1)}, bf16[8,176,1408]{2,1,0:T(8,128)(2,1)S(1)}, u32[]{:S(2)}) copy-start(bf16[8,176,1408]{2,1,0:T(8,128)(2,1)S(1)} %fusion.6) | copy-start | bytes 11894788
  170.4 13.5 %all-to-all-start.2 = ((f32[8,22,256]{2,1,0:T(8,128)}), f32[8,22,256]{2,1,0:T(8,128)S(1)}, u32[]{:S(2)}, u32[]{:S(2)}) async-start(f32[8,22,256]{2,1,0:T(8,128)} %all_to_all.31), calls=%async_computation.3 | async-start | bytes 393216 | tf_op jit(solution)/shard_map/all_to_all | solution.py:77
Sparse Core Ops, SparseCore 0:
  77.1 91.5 reduce-scatter.1
